TPU v7x, 256 devices: a whole 4x4x8 slice. The times are simulated.
256 devices in a mesh: ctx: 8 (over y, x_hi), ch: 32 (over z, x_lo, core).
Axes of the slice: x: 4 (x_hi: 2, x_lo: 2; x = x_hi * 2 + x_lo), y: 4, z: 8, core: 2. Of those that a mesh axis runs over, the one named last changes fastest.
Arguments:
- gate_act: bfloat16 [4096, 8192], P('ctx', 'ch'), may hold values from -6 to 6
- key_act: bfloat16 [4096, 8192], P('ctx', 'ch'), may hold values from -6 to 6
- value_act: bfloat16 [4096, 8192], P('ctx', 'ch'), may hold values from -6 to 6
- filter_taps: float32 [6144, 8192], P('ctx', 'ch'), may hold values from -2 to 2
- skip_gain: float32 [8192], P('ch'), may hold values from 0.5 to 1.5
- w_out: bfloat16 [8192, 8192], P(None, 'ch'), may hold values from -0.0625 to 0.0625
- span_order: int32 [16], replicated, may hold values from 0 to 15, each once
- decode_order: int32 [8], replicated, may hold values from 0 to 7, each once
Outputs:
- projected: bfloat16 [4096, 8192], P('ctx', 'ch')
- tail: float32 [2048, 8192], P('ctx', 'ch')
Inputs may be any that keep to these rules, and one draw needn't show every extreme that they name: `span_order`: each span number once. `decode_order`: each future block number once.
All inputs are finite; a program needn't handle non-finite values.
Results may differ from a plain program's by a relative error of at most 0.017.
Values may be sent and summed in bfloat16 or wider, within the bound.
No kernel may reach another device: no remote copies, remote signals or barrier semaphores. Data moves between devices by JAX's collectives and lax.ppermute only.
A program may use at most 128 MiB of HBM per device.

v0:
```python
import math

import jax
import jax.numpy as jnp
from jax import lax
from jax.experimental import pallas as pl
from jax.experimental.pallas import tpu as pltpu
from jax.sharding import Mesh, PartitionSpec as P


SPAN = 256


HIGH = lax.Precision.HIGH


def forward_table(length):
    half = length // 2
    rows_idx = lax.broadcasted_iota(jnp.int32, (length, length), 0)
    cols_idx = lax.broadcasted_iota(jnp.int32, (length, length), 1)
    frequency = rows_idx % half
    phase = (frequency * cols_idx % length).astype(jnp.float32) * (2.0 * math.pi / length)
    parity = (1 - 2 * (cols_idx % 2)).astype(jnp.float32)
    table = jnp.where(rows_idx < half, jnp.cos(phase), -jnp.sin(phase))
    return jnp.where(rows_idx == half, parity, table)


def inverse_table(length):
    half = length // 2
    rows_idx = lax.broadcasted_iota(jnp.int32, (half, length), 0)
    cols_idx = lax.broadcasted_iota(jnp.int32, (half, length), 1)
    frequency = cols_idx % half
    phase = (frequency * rows_idx % length).astype(jnp.float32) * (2.0 * math.pi / length)
    weight = jnp.where(frequency == 0, 1.0 / length, 2.0 / length)
    table = jnp.where(cols_idx < half, weight * jnp.cos(phase), -weight * jnp.sin(phase))
    parity = (1 - 2 * (rows_idx % 2)).astype(jnp.float32) / length
    return jnp.where(cols_idx == half, parity, table)


def products(seg2d, span2d, lag_idx, lag_ok, n_targets, width, kt=32):
    half = seg2d.shape[0] // 2
    n_slots = span2d.shape[1] // width
    steps = half // kt

    def kernel(lag_ref, ok_ref, seg_re, seg_im, sp_re, sp_im, out_re, out_im):
        row = lax.broadcasted_iota(jnp.int32, (kt, width), 0)
        first = (pl.program_id(0) == 0) & (row == 0)
        for a in range(n_targets):

            def step(i, acc, a=a):
                acc_re, acc_im = acc
                lag = lag_ref[a * n_slots + i]
                w = ok_ref[a * n_slots + i].astype(jnp.float32)
                off = pl.multiple_of(lag * width, width)
                own = pl.multiple_of(i * width, width)
                lr = seg_re[:, pl.ds(off, width)]
                li = seg_im[:, pl.ds(off, width)]
                rr = sp_re[:, pl.ds(own, width)]
                ri = sp_im[:, pl.ds(own, width)]
                cross = li * ri
                re = lr * rr - jnp.where(first, 0.0, cross)
                im = jnp.where(first, cross, lr * ri + li * rr)
                return (acc_re + w * re, acc_im + w * im)

            zero = jnp.zeros((kt, width), jnp.float32)
            acc_re, acc_im = lax.fori_loop(0, n_slots, step, (zero, zero), unroll=4)
            out_re[:, a * width:(a + 1) * width] = acc_re
            out_im[:, a * width:(a + 1) * width] = acc_im

    seg_cols = seg2d.shape[1]
    span_cols = span2d.shape[1]
    grid_spec = pltpu.PrefetchScalarGridSpec(
        num_scalar_prefetch=2,
        grid=(steps,),
        in_specs=[
            pl.BlockSpec((kt, seg_cols), lambda i, l, o: (i, 0)),
            pl.BlockSpec((kt, seg_cols), lambda i, l, o: (i + steps, 0)),
            pl.BlockSpec((kt, span_cols), lambda i, l, o: (i, 0)),
            pl.BlockSpec((kt, span_cols), lambda i, l, o: (i + steps, 0)),
        ],
        out_specs=[
            pl.BlockSpec((kt, n_targets * width), lambda i, l, o: (i, 0)),
            pl.BlockSpec((kt, n_targets * width), lambda i, l, o: (i, 0)),
        ],
    )
    out_shape = [jax.ShapeDtypeStruct((half, n_targets * width), jnp.float32)] * 2
    re, im = pl.pallas_call(kernel, grid_spec=grid_spec, out_shape=out_shape)(
        lag_idx, lag_ok, seg2d, seg2d, span2d, span2d)
    return jnp.concatenate([re, im], axis=0)


def swap(x, axis):
    count = lax.axis_size(axis)
    return lax.ppermute(x, axis, [(i, (i + 1) % count) for i in range(count)])


def channel_part(
    gate_act, key_act, value_act, filter_taps, skip_gain, w_rows, span_order, decode_order, after
):
    width = gate_act.shape[1]
    length = 2 * SPAN
    cycle_size = lax.axis_size("ctx")
    position = lax.axis_index("ctx")
    count_spans = 2 * cycle_size
    count_lags = 3 * cycle_size
    forward = forward_table(length).astype(jnp.bfloat16)
    inverse = inverse_table(length)
    signal = (key_act.astype(jnp.float32) * value_act.astype(jnp.float32)).astype(jnp.bfloat16)

    own = jnp.concatenate([filter_taps.astype(jnp.bfloat16), signal], axis=0)
    forward, inverse, own = lax.optimization_barrier((forward, inverse, own))
    parts = [own] + [
        lax.ppermute(own, "ctx", [(i, (i + shift) % cycle_size) for i in range(cycle_size)])
        for shift in range(1, cycle_size)
    ]
    stacked = jnp.stack(parts)
    if after is not None:
        stacked, _ = lax.optimization_barrier((stacked, after))
    tap_rows = filter_taps.shape[0]
    per_lag = tap_rows // SPAN
    per_span = signal.shape[0] // SPAN
    blocks = stacked[:, :tap_rows].reshape(cycle_size, per_lag, SPAN, width)
    piece = stacked[:, tap_rows:].reshape(cycle_size, per_span, SPAN, width)

    previous = jnp.roll(blocks[:, per_lag - 1 :], -1, axis=0)
    first_part = (jnp.arange(cycle_size) == position)[:, None, None, None]
    previous = jnp.where(first_part, jnp.zeros_like(previous), previous)
    earlier = jnp.concatenate([previous, blocks[:, : per_lag - 1]], axis=1)
    seg_time = jnp.concatenate(
        [
            blocks.transpose(2, 0, 1, 3),
            jnp.zeros((1, cycle_size, per_lag, width), jnp.bfloat16),
            earlier[:, :, 1:].transpose(2, 0, 1, 3),
        ],
        axis=0,
    ).reshape(length, count_lags * width)
    seg_spec = jnp.dot(forward, seg_time, preferred_element_type=jnp.float32)
    span_time = piece.transpose(2, 0, 1, 3).reshape(SPAN, count_spans * width)
    span_spec = jnp.dot(forward[:, :SPAN], span_time, preferred_element_type=jnp.float32)

    held = jnp.arange(count_spans)
    global_slot = per_span * ((position - held // per_span) % cycle_size) + held % per_span
    held_spans = span_order[global_slot]
    my_spans = lax.dynamic_slice_in_dim(span_order, per_span * position, per_span)
    my_future = count_spans + lax.dynamic_index_in_dim(decode_order, position, keepdims=False)
    targets = jnp.concatenate([my_spans, my_future[None]])
    lags = targets[:, None] - held_spans[None, :]
    valid = lags >= 0
    lag = jnp.maximum(lags, 0)
    column = per_lag * ((position - lag // per_lag) % cycle_size) + lag % per_lag
    totals = products(
        seg_spec,
        span_spec,
        column.reshape(-1),
        valid.astype(jnp.int32).reshape(-1),
        targets.shape[0],
        width,
    )
    blocks_out = jnp.dot(inverse, totals, precision=HIGH, preferred_element_type=jnp.float32)
    conv = jnp.concatenate([blocks_out[:, :width], blocks_out[:, width : 2 * width]], axis=0)
    tail = blocks_out[:, 2 * width :]
    mixed = (
        gate_act.astype(jnp.float32) * (conv + skip_gain[None, :] * signal.astype(jnp.float32))
    ).astype(jnp.bfloat16)

    xlo = lax.axis_index("xlo")
    other = swap(mixed, "xlo")
    pair = jnp.where(
        xlo == 0,
        jnp.concatenate([mixed, other], axis=1),
        jnp.concatenate([other, mixed], axis=1),
    )
    ring = lax.all_gather(pair, "z", axis=1, tiled=True)
    w_own, w_other = w_rows
    summed = jnp.dot(ring, w_own, preferred_element_type=jnp.float32) + jnp.dot(
        swap(ring, "core"), w_other, preferred_element_type=jnp.float32
    )
    return summed, tail, mixed


def halves_of(
    gate_act, key_act, value_act, filter_taps, skip_gain, w_out, span_order, decode_order
):
    width = gate_act.shape[1]
    count_z = lax.axis_size("z")
    core = lax.axis_index("core")
    w5 = w_out.reshape(count_z, 2, 2, width, w_out.shape[1])
    w_own_all = lax.dynamic_index_in_dim(w5, core, axis=2, keepdims=False)
    w_other_all = lax.dynamic_index_in_dim(w5, 1 - core, axis=2, keepdims=False)
    halves = 2
    part_width = width // halves
    total = None
    previous = None
    tails = []
    for half in range(halves):
        cols = slice(half * part_width, (half + 1) * part_width)
        rows = count_z * 2 * part_width
        w_rows = (
            w_own_all[:, :, cols].reshape(rows, -1),
            w_other_all[:, :, cols].reshape(rows, -1),
        )
        summed, tail, previous = channel_part(
            gate_act[:, cols],
            key_act[:, cols],
            value_act[:, cols],
            filter_taps[:, cols],
            skip_gain[cols],
            w_rows,
            span_order,
            decode_order,
            previous,
        )
        total = summed if total is None else total + summed
        tails.append(tail)
    projected = total.astype(jnp.bfloat16)
    return (projected, jnp.concatenate(tails, axis=1))


def solution(mesh):
    ch = mesh.shape["ch"]
    fine = Mesh(
        mesh.devices.reshape(mesh.shape["ctx"], ch // 4, 2, 2), ("ctx", "z", "xlo", "core")
    )
    chans = ("z", "xlo", "core")
    in_specs = (
        P("ctx", chans),
        P("ctx", chans),
        P("ctx", chans),
        P("ctx", chans),
        P(chans),
        P(None, chans),
        P(),
        P(),
    )
    out_specs = (P("ctx", chans), P("ctx", chans))
    return jax.shard_map(
        halves_of, mesh=fine, in_specs=in_specs, out_specs=out_specs, check_vma=False
    )
```

profile of v0, /device:TPU:1, one launch (start us, length us, event | category | flops | bytes accessed | tf_op | source)
XLA Modules:
  0.0 267.2 jit_solution(653029177154603317)
XLA Ops:
  10.4 5.7 %select_convert_fusion = bf16[512,512]{1,0:T(8,128)(2,1)} fusion(s32[512]{0:T(512)S(1)} %get-tuple-element.46, s32[512]{0:T(512)S(1)} %get-tuple-element.47, s32[512]{0:T(512)S(1)} %get-tuple-element.50, s32[512]{0:T(512)S(1)} %get-tuple-element.51, pred[512]{0:T(512)(128)(4,1)S(1)} %get-tuple-element.53, pred[512]{0:T(512)(128)(4,1)S(1)} %get-tuple-element.48, ...), kind=kLoop, calls=%fused_computation.19 | loop fusion | flops 6029312 | bytes 534528 | tf_op jit(solution)/shard_map/convert_element_type | solution.py:106
  16.1 3.0 %fusion.16 = f32[256,512]{1,0:T(8,128)} fusion(s32[512]{0:T(512)S(1)} %get-tuple-element.46, s32[512]{0:T(512)S(1)} %get-tuple-element.47, s32[256]{0:T(256)S(1)} %get-tuple-element.54, s32[256]{0:T(256)S(1)} %get-tuple-element.55, pred[256]{0:T(512)(128)(4,1)S(1)} %compare_and_fusion, pred[512]{0:T(512)(128)(4,1)S(1)} %get-tuple-element.53, ...), kind=kLoop, calls=%fused_computation.36 | loop fusion | flops 3538944 | bytes 532224 | tf_op jit(solution)/shard_map/jit(_where)/select_n | solution.py:37
  19.1 3.6 %collective-permute-start = (bf16[1280,128]{1,0:T(8,128)(2,1)S(1)}, bf16[1280,128]{1,0:T(8,128)(2,1)}, u32[]{:S(2)}, u32[]{:S(2)}) collective-permute-start(bf16[1280,128]{1,0:T(8,128)(2,1)S(1)} %pad_maximum_fusion.4), channel_id=1, source_target_pairs={{0,32},{32,64},{64,96},{96,128},{128,160},{160,192},{192,224},{224... | collective-permute-start | bytes 983048 | tf_op jit(solution)/shard_map/ppermute | solution.py:113
  27.5 4.5 %collective-permute-start.4 = (bf16[1280,128]{1,0:T(8,128)(2,1)S(1)}, bf16[1280,128]{1,0:T(8,128)(2,1)}, u32[]{:S(2)}, u32[]{:S(2)}) collective-permute-start(bf16[1280,128]{1,0:T(8,128)(2,1)S(1)} %pad_maximum_fusion.4), channel_id=1, source_target_pairs={{0,160},{32,192},{64,224},{96,0},{128,32},{160,64},{192,96},{224,1... | collective-permute-start | bytes 983048 | tf_op jit(solution)/shard_map/ppermute | solution.py:113
  39.7 7.7 %collective-permute-done.1 = bf16[1280,128]{1,0:T(8,128)(2,1)} collective-permute-done((bf16[1280,128]{1,0:T(8,128)(2,1)S(1)}, bf16[1280,128]{1,0:T(8,128)(2,1)}, u32[]{:S(2)}, u32[]{:S(2)}) %collective-permute-start.1) | collective-permute-done | bytes 327712 | tf_op jit(solution)/shard_map/ppermute | solution.py:113
  48.4 3.0 %collective-permute-start.9 = (bf16[1280,128]{1,0:T(8,128)(2,1)S(1)}, bf16[1280,128]{1,0:T(8,128)(2,1)}, u32[]{:S(2)}, u32[]{:S(2)}) collective-permute-start(bf16[1280,128]{1,0:T(8,128)(2,1)S(1)} %pad_maximum_fusion.5), channel_id=1, source_target_pairs={{0,32},{32,64},{64,96},{96,128},{128,160},{160,192},{192,224},{224... | collective-permute-start | bytes 983048 | tf_op jit(solution)/shard_map/ppermute | solution.py:113
  52.5 3.0 %collective-permute-done.3 = bf16[1280,128]{1,0:T(8,128)(2,1)} collective-permute-done((bf16[1280,128]{1,0:T(8,128)(2,1)S(1)}, bf16[1280,128]{1,0:T(8,128)(2,1)}, u32[]{:S(2)}, u32[]{:S(2)}) %collective-permute-start.3) | collective-permute-done | bytes 327712 | tf_op jit(solution)/shard_map/ppermute | solution.py:113
  57.7 2.7 %collective-permute-start.12 = (bf16[1280,128]{1,0:T(8,128)(2,1)S(1)}, bf16[1280,128]{1,0:T(8,128)(2,1)}, u32[]{:S(2)}, u32[]{:S(2)}) collective-permute-start(bf16[1280,128]{1,0:T(8,128)(2,1)S(1)} %pad_maximum_fusion.5), channel_id=1, source_target_pairs={{0,128},{32,160},{64,192},{96,224},{128,0},{160,32},{192,64},{224,... | collective-permute-start | bytes 983048 | tf_op jit(solution)/shard_map/ppermute | solution.py:113
  60.5 3.4 %collective-permute-start.13 = (bf16[1280,128]{1,0:T(8,128)(2,1)S(1)}, bf16[1280,128]{1,0:T(8,128)(2,1)}, u32[]{:S(2)}, u32[]{:S(2)}) collective-permute-start(bf16[1280,128]{1,0:T(8,128)(2,1)S(1)} %pad_maximum_fusion.5), channel_id=1, source_target_pairs={{0,160},{32,192},{64,224},{96,0},{128,32},{160,64},{192,96},{224,1... | collective-permute-start | bytes 983048 | tf_op jit(solution)/shard_map/ppermute | solution.py:113
  68.5 3.2 %copy.10 = bf16[512,8,3,128]{0,3,2,1:T(8,128)(2,1)S(1)} copy(bf16[512,8,3,128]{3,0,2,1:T(8,128)(2,1)} %pad_maximum_fusion) | data formatting | bytes 6291456 | tf_op jit(solution)/shard_map/concatenate | solution.py:129
  73.9 5.5 %fusion.59.seg_re.seg_im = f32[512,3072]{1,0:T(8,128)} fusion(bf16[512,512]{1,0:T(8,128)(2,1)} %select_convert_fusion, bf16[512,3072]{0,1:T(8,128)(2,1)S(1)} %bitcast.88), kind=kOutput, calls=%fused_computation.131 | convolution fusion | flops 1610612736 | bytes 9961472 | tf_op jit(solution)/shard_map/dot_general | solution.py:137
  83.6 3.3 %collective-permute-done.10 = bf16[1280,128]{1,0:T(8,128)(2,1)} collective-permute-done((bf16[1280,128]{1,0:T(8,128)(2,1)S(1)}, bf16[1280,128]{1,0:T(8,128)(2,1)}, u32[]{:S(2)}, u32[]{:S(2)}) %collective-permute-start.10) | collective-permute-done | bytes 327712 | tf_op jit(solution)/shard_map/ppermute | solution.py:113
  93.7 2.8 %fusion.27.sp_re.sp_im = f32[512,2048]{1,0:T(8,128)} fusion(bf16[256,2048]{0,1:T(8,128)(2,1)S(1)} %bitcast.93, bf16[512,512]{1,0:T(8,128)(2,1)S(1)} %copy-done.3), kind=kOutput, calls=%fused_computation.73 | convolution fusion | flops 536870912 | bytes 5505024 | tf_op jit(solution)/shard_map/dot_general | solution.py:139
  96.6 9.7 %shard_map.95 = (f32[256,384]{1,0:T(8,128)}, f32[256,384]{1,0:T(8,128)}) custom-call(s32[48]{0:T(128)} %fusion.44.lag_ref, s32[48]{0:T(128)} %reshape.247.ok_ref, f32[512,3072]{1,0:T(8,128)} %fusion.59.seg_re.seg_im, f32[512,3072]{1,0:T(8,128)} %fusion.59.seg_re.seg_im, f32[512,2048]{1,0:T(8,128)} %fusion.27.sp_re.sp_im, f32[512,2048]{1,0:T(8,128)} %fusion.27.sp_re.sp_im), custom_call_target="tpu_custom_call" | custom-call | tf_op jit(solution)/shard_map/pallas_call | solution.py:87
  116.0 3.2 %copy.12 = bf16[512,8,3,128]{0,3,2,1:T(8,128)(2,1)S(1)} copy(bf16[512,8,3,128]{3,0,2,1:T(8,128)(2,1)} %pad_maximum_fusion.1) | data formatting | bytes 6291456 | tf_op jit(solution)/shard_map/concatenate | solution.py:129
  121.5 5.7 %fusion.61.seg_re.seg_im = f32[512,3072]{1,0:T(8,128)} fusion(bf16[512,512]{1,0:T(8,128)(2,1)} %select_convert_fusion, bf16[512,3072]{0,1:T(8,128)(2,1)S(1)} %bitcast.89), kind=kOutput, calls=%fused_computation.133 | convolution fusion | flops 1610612736 | bytes 9961472 | tf_op jit(solution)/shard_map/dot_general | solution.py:137
  127.1 2.8 %fusion.25.sp_re.sp_im = f32[512,2048]{1,0:T(8,128)} fusion(bf16[256,2048]{0,1:T(8,128)(2,1)S(1)} %bitcast.94, bf16[512,512]{1,0:T(8,128)(2,1)S(1)} %copy-done.4), kind=kOutput, calls=%fused_computation.70 | convolution fusion | flops 536870912 | bytes 5505024 | tf_op jit(solution)/shard_map/dot_general | solution.py:139
  130.0 9.5 %shard_map.96 = (f32[256,384]{1,0:T(8,128)}, f32[256,384]{1,0:T(8,128)}) custom-call(s32[48]{0:T(128)} %fusion.44.lag_ref, s32[48]{0:T(128)} %reshape.247.ok_ref, f32[512,3072]{1,0:T(8,128)} %fusion.61.seg_re.seg_im, f32[512,3072]{1,0:T(8,128)} %fusion.61.seg_re.seg_im, f32[512,2048]{1,0:T(8,128)} %fusion.25.sp_re.sp_im, f32[512,2048]{1,0:T(8,128)} %fusion.25.sp_re.sp_im), custom_call_target="tpu_custom_call" | custom-call | tf_op jit(solution)/shard_map/pallas_call | solution.py:87
  141.5 3.8 %collective-permute-done.16 = bf16[512,128]{1,0:T(8,128)(2,1)S(1)} collective-permute-done((bf16[512,128]{1,0:T(8,128)(2,1)S(1)}, bf16[512,128]{1,0:T(8,128)(2,1)S(1)}, u32[]{:S(2)}, u32[]{:S(2)}) %collective-permute-start.16) | collective-permute-done | bytes 131104 | tf_op jit(solution)/shard_map/ppermute | solution.py:94
  146.2 5.3 %collective-permute-done.7 = bf16[512,128]{1,0:T(8,128)(2,1)S(1)} collective-permute-done((bf16[512,128]{1,0:T(8,128)(2,1)S(1)}, bf16[512,128]{1,0:T(8,128)(2,1)S(1)}, u32[]{:S(2)}, u32[]{:S(2)}) %collective-permute-start.7) | collective-permute-done | bytes 131104 | tf_op jit(solution)/shard_map/ppermute | solution.py:94
  152.4 43.5 %all-gather.5.cloned.1.call-done = bf16[512,2048]{1,0:T(8,128)(2,1)} async-done(((bf16[512,256]{1,0:T(8,128)(2,1)}), bf16[512,2048]{1,0:T(8,128)(2,1)}) %all-gather.5.cloned.1.call-update) | async-done | bytes 2097168 | tf_op jit(solution)/shard_map/all_gather | solution.py:173
  195.9 5.5 %collective-permute-start.17 = (bf16[512,2048]{1,0:T(8,128)(2,1)}, bf16[512,2048]{1,0:T(8,128)(2,1)S(1)}, u32[]{:S(2)}, u32[]{:S(2)}) collective-permute-start(bf16[512,2048]{1,0:T(8,128)(2,1)} %all-gather.5.cloned.1.call-done), channel_id=1, source_target_pairs={{0,1},{1,0},{2,3},{3,2},{4,5},{5,4},{6,7},{7,6},{8,9},{9,8},{10,11... | collective-permute-start | bytes 6291464 | tf_op jit(solution)/shard_map/ppermute | solution.py:94
  201.4 43.0 %all-gather.3.cloned.1.call-done = bf16[512,2048]{1,0:T(8,128)(2,1)} async-done(((bf16[512,256]{1,0:T(8,128)(2,1)}), bf16[512,2048]{1,0:T(8,128)(2,1)}) %all-gather.3.cloned.1.call-update) | async-done | bytes 2097168 | tf_op jit(solution)/shard_map/all_gather | solution.py:173
  244.4 5.5 %collective-permute-start.8 = (bf16[512,2048]{1,0:T(8,128)(2,1)}, bf16[512,2048]{1,0:T(8,128)(2,1)}, u32[]{:S(2)}, u32[]{:S(2)}) collective-permute-start(bf16[512,2048]{1,0:T(8,128)(2,1)} %all-gather.3.cloned.1.call-done), channel_id=1, source_target_pairs={{0,1},{1,0},{2,3},{3,2},{4,5},{5,4},{6,7},{7,6},{8,9},{9,8},{10,11... | collective-permute-start | bytes 6291464 | tf_op jit(solution)/shard_map/ppermute | solution.py:94
  (144 shorter events, 63.1 us)
Async XLA Ops:
  7.2 188.8 %all-gather.5.cloned.1.call-start = ((), (), s32[]{:S(2)}) async-start(), calls=%async_computation.1 | async-start | bytes 2359296 | tf_op jit(solution)/shard_map/all_gather | solution.py:173
  7.3 24.7 %copy-start = (s32[16]{0:T(128)S(1)}, s32[16]{0:T(128)}, u32[]{:S(2)}) copy-start(s32[16]{0:T(128)} %param.14) | copy-start | bytes 196
  8.5 24.3 %copy-start.19 = (s32[8]{0:T(128)S(1)}, s32[8]{0:T(128)}, u32[]{:S(2)}) copy-start(s32[8]{0:T(128)} %param.15) | copy-start | bytes 100
  8.5 26.8 %copy-start.16 = (f32[256]{0:T(256)S(1)}, f32[256]{0:T(256)}, u32[]{:S(2)}) copy-start(f32[256]{0:T(256)} %param.12) | copy-start | bytes 3076
  10.4 29.3 %copy-start.8 = (bf16[512,128]{1,0:T(8,128)(2,1)}, bf16[512,128]{1,0:T(8,128)(2,1)S(1)}, u32[]{:S(2)}) copy-start(bf16[512,128]{1,0:T(8,128)(2,1)S(1)} %get-tuple-element.30) | copy-start | bytes 393220
  19.1 18.5 %collective-permute-start = (bf16[1280,128]{1,0:T(8,128)(2,1)S(1)}, bf16[1280,128]{1,0:T(8,128)(2,1)}, u32[]{:S(2)}, u32[]{:S(2)}) collective-permute-start(bf16[1280,128]{1,0:T(8,128)(2,1)S(1)} %pad_maximum_fusion.4), channel_id=1, source_target_pairs={{0,32},{32,64},{64,96},{96,128},{128,160},{160,192},{192,224},{224... | collective-permute-start | bytes 983048 | tf_op jit(solution)/shard_map/ppermute | solution.py:113
  22.6 24.8 %collective-permute-start.1 = (bf16[1280,128]{1,0:T(8,128)(2,1)S(1)}, bf16[1280,128]{1,0:T(8,128)(2,1)}, u32[]{:S(2)}, u32[]{:S(2)}) collective-permute-start(bf16[1280,128]{1,0:T(8,128)(2,1)S(1)} %pad_maximum_fusion.4), channel_id=1, source_target_pairs={{0,64},{32,96},{64,128},{96,160},{128,192},{160,224},{192,0},{224,... | collective-permute-start | bytes 983048 | tf_op jit(solution)/shard_map/ppermute | solution.py:113
  23.9 24.5 %collective-permute-start.2 = (bf16[1280,128]{1,0:T(8,128)(2,1)S(1)}, bf16[1280,128]{1,0:T(8,128)(2,1)}, u32[]{:S(2)}, u32[]{:S(2)}) collective-permute-start(bf16[1280,128]{1,0:T(8,128)(2,1)S(1)} %pad_maximum_fusion.4), channel_id=1, source_target_pairs={{0,96},{32,128},{64,160},{96,192},{128,224},{160,0},{192,32},{224,... | collective-permute-start | bytes 983048 | tf_op jit(solution)/shard_map/ppermute | solution.py:113
  25.9 29.7 %collective-permute-start.3 = (bf16[1280,128]{1,0:T(8,128)(2,1)S(1)}, bf16[1280,128]{1,0:T(8,128)(2,1)}, u32[]{:S(2)}, u32[]{:S(2)}) collective-permute-start(bf16[1280,128]{1,0:T(8,128)(2,1)S(1)} %pad_maximum_fusion.4), channel_id=1, source_target_pairs={{0,128},{32,160},{64,192},{96,224},{128,0},{160,32},{192,64},{224,... | collective-permute-start | bytes 983048 | tf_op jit(solution)/shard_map/ppermute | solution.py:113
  27.5 29.1 %collective-permute-start.4 = (bf16[1280,128]{1,0:T(8,128)(2,1)S(1)}, bf16[1280,128]{1,0:T(8,128)(2,1)}, u32[]{:S(2)}, u32[]{:S(2)}) collective-permute-start(bf16[1280,128]{1,0:T(8,128)(2,1)S(1)} %pad_maximum_fusion.4), channel_id=1, source_target_pairs={{0,160},{32,192},{64,224},{96,0},{128,32},{160,64},{192,96},{224,1... | collective-permute-start | bytes 983048 | tf_op jit(solution)/shard_map/ppermute | solution.py:113
  37.6 20.1 %collective-permute-start.5 = (bf16[1280,128]{1,0:T(8,128)(2,1)S(1)}, bf16[1280,128]{1,0:T(8,128)(2,1)S(1)}, u32[]{:S(2)}, u32[]{:S(2)}) collective-permute-start(bf16[1280,128]{1,0:T(8,128)(2,1)S(1)} %pad_maximum_fusion.4), channel_id=1, source_target_pairs={{0,192},{32,224},{64,0},{96,32},{128,64},{160,96},{192,128},{224,1... | collective-permute-start | bytes 983048 | tf_op jit(solution)/shard_map/ppermute | solution.py:113
  47.4 13.1 %collective-permute-start.6 = (bf16[1280,128]{1,0:T(8,128)(2,1)S(1)}, bf16[1280,128]{1,0:T(8,128)(2,1)S(1)}, u32[]{:S(2)}, u32[]{:S(2)}) collective-permute-start(bf16[1280,128]{1,0:T(8,128)(2,1)S(1)} %pad_maximum_fusion.4), channel_id=1, source_target_pairs={{0,224},{32,0},{64,32},{96,64},{128,96},{160,128},{192,160},{224,1... | collective-permute-start | bytes 983048 | tf_op jit(solution)/shard_map/ppermute | solution.py:113
  48.4 31.0 %collective-permute-start.9 = (bf16[1280,128]{1,0:T(8,128)(2,1)S(1)}, bf16[1280,128]{1,0:T(8,128)(2,1)}, u32[]{:S(2)}, u32[]{:S(2)}) collective-permute-start(bf16[1280,128]{1,0:T(8,128)(2,1)S(1)} %pad_maximum_fusion.5), channel_id=1, source_target_pairs={{0,32},{32,64},{64,96},{96,128},{128,160},{160,192},{192,224},{224... | collective-permute-start | bytes 983048 | tf_op jit(solution)/shard_map/ppermute | solution.py:113
  55.6 31.3 %collective-permute-start.10 = (bf16[1280,128]{1,0:T(8,128)(2,1)S(1)}, bf16[1280,128]{1,0:T(8,128)(2,1)}, u32[]{:S(2)}, u32[]{:S(2)}) collective-permute-start(bf16[1280,128]{1,0:T(8,128)(2,1)S(1)} %pad_maximum_fusion.5), channel_id=1, source_target_pairs={{0,64},{32,96},{64,128},{96,160},{128,192},{160,224},{192,0},{224,... | collective-permute-start | bytes 983048 | tf_op jit(solution)/shard_map/ppermute | solution.py:113
  56.6 31.9 %collective-permute-start.11 = (bf16[1280,128]{1,0:T(8,128)(2,1)S(1)}, bf16[1280,128]{1,0:T(8,128)(2,1)}, u32[]{:S(2)}, u32[]{:S(2)}) collective-permute-start(bf16[1280,128]{1,0:T(8,128)(2,1)S(1)} %pad_maximum_fusion.5), channel_id=1, source_target_pairs={{0,96},{32,128},{64,160},{96,192},{128,224},{160,0},{192,32},{224,... | collective-permute-start | bytes 983048 | tf_op jit(solution)/shard_map/ppermute | solution.py:113
  57.7 32.5 %collective-permute-start.12 = (bf16[1280,128]{1,0:T(8,128)(2,1)S(1)}, bf16[1280,128]{1,0:T(8,128)(2,1)}, u32[]{:S(2)}, u32[]{:S(2)}) collective-permute-start(bf16[1280,128]{1,0:T(8,128)(2,1)S(1)} %pad_maximum_fusion.5), channel_id=1, source_target_pairs={{0,128},{32,160},{64,192},{96,224},{128,0},{160,32},{192,64},{224,... | collective-permute-start | bytes 983048 | tf_op jit(solution)/shard_map/ppermute | solution.py:113
  60.5 31.5 %collective-permute-start.13 = (bf16[1280,128]{1,0:T(8,128)(2,1)S(1)}, bf16[1280,128]{1,0:T(8,128)(2,1)}, u32[]{:S(2)}, u32[]{:S(2)}) collective-permute-start(bf16[1280,128]{1,0:T(8,128)(2,1)S(1)} %pad_maximum_fusion.5), channel_id=1, source_target_pairs={{0,160},{32,192},{64,224},{96,0},{128,32},{160,64},{192,96},{224,1... | collective-permute-start | bytes 983048 | tf_op jit(solution)/shard_map/ppermute | solution.py:113
  79.5 28.6 %collective-permute-start.14 = (bf16[1280,128]{1,0:T(8,128)(2,1)S(1)}, bf16[1280,128]{1,0:T(8,128)(2,1)}, u32[]{:S(2)}, u32[]{:S(2)}) collective-permute-start(bf16[1280,128]{1,0:T(8,128)(2,1)S(1)} %pad_maximum_fusion.5), channel_id=1, source_target_pairs={{0,192},{32,224},{64,0},{96,32},{128,64},{160,96},{192,128},{224,1... | collective-permute-start | bytes 983048 | tf_op jit(solution)/shard_map/ppermute | solution.py:113
  86.8 23.6 %collective-permute-start.15 = (bf16[1280,128]{1,0:T(8,128)(2,1)S(1)}, bf16[1280,128]{1,0:T(8,128)(2,1)}, u32[]{:S(2)}, u32[]{:S(2)}) collective-permute-start(bf16[1280,128]{1,0:T(8,128)(2,1)S(1)} %pad_maximum_fusion.5), channel_id=1, source_target_pairs={{0,224},{32,0},{64,32},{96,64},{128,96},{160,128},{192,160},{224,1... | collective-permute-start | bytes 983048 | tf_op jit(solution)/shard_map/ppermute | solution.py:113
  141.4 3.9 %collective-permute-start.16 = (bf16[512,128]{1,0:T(8,128)(2,1)S(1)}, bf16[512,128]{1,0:T(8,128)(2,1)S(1)}, u32[]{:S(2)}, u32[]{:S(2)}) collective-permute-start(bf16[512,128]{1,0:T(8,128)(2,1)S(1)} %fusion.24), channel_id=1, source_target_pairs={{0,2},{2,0},{1,3},{3,1},{4,6},{6,4},{5,7},{7,5},{8,10},{10,8},{9,1... | collective-permute-start | bytes 393224 | tf_op jit(solution)/shard_map/ppermute | solution.py:94
  146.1 98.3 %all-gather.3.cloned.1.call-start = ((), (), s32[]{:S(2)}) async-start(), calls=%async_computation | async-start | bytes 2359296 | tf_op jit(solution)/shard_map/all_gather | solution.py:173
  146.1 5.5 %collective-permute-start.7 = (bf16[512,128]{1,0:T(8,128)(2,1)S(1)}, bf16[512,128]{1,0:T(8,128)(2,1)S(1)}, u32[]{:S(2)}, u32[]{:S(2)}) collective-permute-start(bf16[512,128]{1,0:T(8,128)(2,1)S(1)} %copy-done.12), channel_id=1, source_target_pairs={{0,2},{2,0},{1,3},{3,1},{4,6},{6,4},{5,7},{7,5},{8,10},{10,8},{9,1... | collective-permute-start | bytes 393224 | tf_op jit(solution)/shard_map/ppermute | solution.py:94
  195.9 58.2 %collective-permute-start.17 = (bf16[512,2048]{1,0:T(8,128)(2,1)}, bf16[512,2048]{1,0:T(8,128)(2,1)S(1)}, u32[]{:S(2)}, u32[]{:S(2)}) collective-permute-start(bf16[512,2048]{1,0:T(8,128)(2,1)} %all-gather.5.cloned.1.call-done), channel_id=1, source_target_pairs={{0,1},{1,0},{2,3},{3,2},{4,5},{5,4},{6,7},{7,6},{8,9},{9,8},{10,11... | collective-permute-start | bytes 6291464 | tf_op jit(solution)/shard_map/ppermute | solution.py:94
  244.4 10.5 %collective-permute-start.8 = (bf16[512,2048]{1,0:T(8,128)(2,1)}, bf16[512,2048]{1,0:T(8,128)(2,1)}, u32[]{:S(2)}, u32[]{:S(2)}) collective-permute-start(bf16[512,2048]{1,0:T(8,128)(2,1)} %all-gather.3.cloned.1.call-done), channel_id=1, source_target_pairs={{0,1},{1,0},{2,3},{3,2},{4,5},{5,4},{6,7},{7,6},{8,9},{9,8},{10,11... | collective-permute-start | bytes 6291464 | tf_op jit(solution)/shard_map/ppermute | solution.py:94
  (16 other events, 128.9 us)
Sparse Core Ops, SparseCore 0:
  146.2 49.6 all-gather.4
  198.2 46.1 all-gather.2
where the time goes:
time: 268 us; the launch traced here: 267 us
  waiting for transfers between devices  110 us (41%)
  local copies, waits for them, and re-layouts  38.2 us (14%)
  starting transfers between devices  36.7 us (14%)
  matrix products  25.6 us (10%)
  other arithmetic  22.5 us (8%)
  Pallas kernels  19.2 us (7%)
  between operations  15.3 us (6%)
    all_gather x2, waiting for transfers between devices, channel_part(): ring = lax.all_gather(pair, 'z', axis=1, tiled=True)  86.5 us
    ppermute x14, starting transfers between devices, channel_part(): lax.ppermute(own, 'ctx', [(i, (i + shift) % cycle_size) for i in range(cy...  25.5 us
    pallas_call x2, Pallas kernels, products(): pl.pallas_call(kernel, grid_spec=grid_spec, out_shape=out_shape)  19.2 us
    unnamed x54, local copies, waits for them, and re-layouts  16.9 us
    ppermute x14, waiting for transfers between devices, channel_part(): lax.ppermute(own, 'ctx', [(i, (i + shift) % cycle_size) for i in range(cy...  14.1 us
    dot_general x2, matrix products, channel_part(): seg_spec = jnp.dot(forward, seg_time, preferred_element_type=jnp.float32)  11.2 us
    ppermute x4, starting transfers between devices, swap(): return lax.ppermute(x, axis, [(i, (i + 1) % count) for i in range(count)])  11.1 us
    ppermute x4, waiting for transfers between devices, swap(): return lax.ppermute(x, axis, [(i, (i + 1) % count) for i in range(count)])  9.15 us
  transfers between devices with their start and end apart: 20, of which 7 were waited for; matrix products, arithmetic and copies ran while one was open for 17% of the time, Pallas kernels for 4%

commit v1 on v0

--- a/solution.py
+++ b/solution.py
@@ -95,7 +95,7 @@
 
 
 def channel_part(
-    gate_act, key_act, value_act, filter_taps, skip_gain, w_rows, span_order, decode_order, after
+    gate_act, key_act, value_act, filter_taps, skip_gain, span_order, decode_order, before, after
 ):
     width = gate_act.shape[1]
     length = 2 * SPAN
@@ -109,6 +109,8 @@
 
     own = jnp.concatenate([filter_taps.astype(jnp.bfloat16), signal], axis=0)
     forward, inverse, own = lax.optimization_barrier((forward, inverse, own))
+    if before is not None:
+        own, _ = lax.optimization_barrier((own, before))
     parts = [own] + [
         lax.ppermute(own, "ctx", [(i, (i + shift) % cycle_size) for i in range(cycle_size)])
         for shift in range(1, cycle_size)
@@ -163,19 +165,7 @@
         gate_act.astype(jnp.float32) * (conv + skip_gain[None, :] * signal.astype(jnp.float32))
     ).astype(jnp.bfloat16)
 
-    xlo = lax.axis_index("xlo")
-    other = swap(mixed, "xlo")
-    pair = jnp.where(
-        xlo == 0,
-        jnp.concatenate([mixed, other], axis=1),
-        jnp.concatenate([other, mixed], axis=1),
-    )
-    ring = lax.all_gather(pair, "z", axis=1, tiled=True)
-    w_own, w_other = w_rows
-    summed = jnp.dot(ring, w_own, preferred_element_type=jnp.float32) + jnp.dot(
-        swap(ring, "core"), w_other, preferred_element_type=jnp.float32
-    )
-    return summed, tail, mixed
+    return tail, mixed, stacked
 
 
 def halves_of(
@@ -184,35 +174,45 @@
     width = gate_act.shape[1]
     count_z = lax.axis_size("z")
     core = lax.axis_index("core")
+    xlo = lax.axis_index("xlo")
     w5 = w_out.reshape(count_z, 2, 2, width, w_out.shape[1])
-    w_own_all = lax.dynamic_index_in_dim(w5, core, axis=2, keepdims=False)
-    w_other_all = lax.dynamic_index_in_dim(w5, 1 - core, axis=2, keepdims=False)
+    rows = count_z * 2 * width
+    w_own = lax.dynamic_index_in_dim(w5, core, axis=2, keepdims=False).reshape(rows, -1)
+    w_other = lax.dynamic_index_in_dim(w5, 1 - core, axis=2, keepdims=False).reshape(rows, -1)
     halves = 2
     part_width = width // halves
-    total = None
+    received = None
     previous = None
     tails = []
+    mixes = []
     for half in range(halves):
         cols = slice(half * part_width, (half + 1) * part_width)
-        rows = count_z * 2 * part_width
-        w_rows = (
-            w_own_all[:, :, cols].reshape(rows, -1),
-            w_other_all[:, :, cols].reshape(rows, -1),
-        )
-        summed, tail, previous = channel_part(
+        tail, previous, received = channel_part(
             gate_act[:, cols],
             key_act[:, cols],
             value_act[:, cols],
             filter_taps[:, cols],
             skip_gain[cols],
-            w_rows,
             span_order,
             decode_order,
+            received,
             previous,
         )
-        total = summed if total is None else total + summed
         tails.append(tail)
-    projected = total.astype(jnp.bfloat16)
+        mixes.append(previous)
+    mixed = jnp.concatenate(mixes, axis=1)
+
+    other = swap(mixed, "xlo")
+    pair = jnp.where(
+        xlo == 0,
+        jnp.concatenate([mixed, other], axis=1),
+        jnp.concatenate([other, mixed], axis=1),
+    )
+    ring = lax.all_gather(pair, "z", axis=1, tiled=True)
+    summed = jnp.dot(ring, w_own, preferred_element_type=jnp.float32) + jnp.dot(
+        swap(ring, "core"), w_other, preferred_element_type=jnp.float32
+    )
+    projected = summed.astype(jnp.bfloat16)
     return (projected, jnp.concatenate(tails, axis=1))
 
 

time: 268 us -> 252 us (0.940)
  starting transfers between devices: 36.7 us -> 24 us
  local copies, waits for them, and re-layouts: 38.2 us -> 31.8 us
  waiting for transfers between devices: 110 us -> 114 us
    ppermute x14, waiting for transfers between devices: 14.1 us -> 43.8 us  [channel_part(): lax.ppermute(own, 'ctx', [(i, (i + shift) % cycle_size) for i in range(cy...]
    all_gather x2 -> x1, waiting for transfers between devices: 86.5 us -> 61.6 us  [halves_of(): ring = lax.all_gather(pair, 'z', axis=1, tiled=True)]
    ppermute x4 -> x2, starting transfers between devices: 11.1 us -> 0.97 us  [swap(): return lax.ppermute(x, axis, [(i, (i + 1) % count) for i in range(count)])]
    unnamed x54, local copies, waits for them, and re-layouts: 16.9 us -> 9.16 us
    dynamic_slice x0 -> x1, local copies, waits for them, and re-layouts: none -> 2.69 us  [halves_of(): lax.dynamic_index_in_dim(w5, core, axis=2, keepdims=False).reshape(rows, -1)]
    ppermute x4 -> x2, waiting for transfers between devices: 9.15 us -> 8.87 us  [swap(): return lax.ppermute(x, axis, [(i, (i + 1) % count) for i in range(count)])]
    dot_general x4 -> x2, matrix products: 5.29 us -> 5.55 us  [the longest x1 3.6 us: halves_of(): jnp.dot(swap(ring, 'core'), w_other, preferred_element_type=jnp.float32)]
  transfers between devices with their start and end apart: 20 -> 17, of which waited for: 7 -> 8; matrix products, arithmetic and copies ran while one was open for 17% -> 15% of each run, Pallas kernels for 4% -> 4%
where the time goes in v1:
time: 252 us; the launch traced here: 251 us
  waiting for transfers between devices  114 us (45%)
  local copies, waits for them, and re-layouts  31.8 us (13%)
  matrix products  26.1 us (10%)
  starting transfers between devices  24 us (10%)
  other arithmetic  20.9 us (8%)
  Pallas kernels  19.1 us (8%)
  between operations  15.2 us (6%)
    all_gather x1, waiting for transfers between devices, halves_of(): ring = lax.all_gather(pair, 'z', axis=1, tiled=True)  61.6 us
    ppermute x14, waiting for transfers between devices, channel_part(): lax.ppermute(own, 'ctx', [(i, (i + shift) % cycle_size) for i in range(cy...  43.8 us
    ppermute x14, starting transfers between devices, channel_part(): lax.ppermute(own, 'ctx', [(i, (i + shift) % cycle_size) for i in range(cy...  23 us
    pallas_call x2, Pallas kernels, products(): pl.pallas_call(kernel, grid_spec=grid_spec, out_shape=out_shape)  19.1 us
    dot_general x2, matrix products, channel_part(): seg_spec = jnp.dot(forward, seg_time, preferred_element_type=jnp.float32)  11.3 us
    unnamed x54, local copies, waits for them, and re-layouts  9.16 us
    ppermute x2, waiting for transfers between devices, swap(): return lax.ppermute(x, axis, [(i, (i + 1) % count) for i in range(count)])  8.87 us
    concatenate x3, local copies, waits for them, and re-layouts, channel_part(): jnp.concatenate([blocks.transpose(2, 0, 1, 3), jnp.zeros((1, cycle_size,...  6.36 us
  transfers between devices with their start and end apart: 17, of which 8 were waited for; matrix products, arithmetic and copies ran while one was open for 15% of the time, Pallas kernels for 4%

profile of v1, /device:TPU:1, one launch (start us, length us, event | category | flops | bytes accessed | tf_op | source)
XLA Modules:
  0.0 251.4 jit_solution(805007986242783032)
XLA Ops:
  9.7 5.7 %select_convert_fusion = bf16[512,512]{1,0:T(8,128)(2,1)} fusion(s32[512]{0:T(512)S(1)} %get-tuple-element.44, s32[512]{0:T(512)S(1)} %get-tuple-element.45, s32[512]{0:T(512)S(1)} %get-tuple-element.48, s32[512]{0:T(512)S(1)} %get-tuple-element.49, pred[512]{0:T(512)(128)(4,1)S(1)} %get-tuple-element.51, pred[512]{0:T(512)(128)(4,1)S(1)} %get-tuple-element.46, ...), kind=kLoop, calls=%fused_computation.15 | loop fusion | flops 6029312 | bytes 534528 | tf_op jit(solution)/shard_map/convert_element_type | solution.py:106
  15.4 3.0 %fusion.15 = f32[256,512]{1,0:T(8,128)} fusion(s32[512]{0:T(512)S(1)} %get-tuple-element.44, s32[512]{0:T(512)S(1)} %get-tuple-element.45, s32[256]{0:T(256)S(1)} %get-tuple-element.52, s32[256]{0:T(256)S(1)} %get-tuple-element.53, pred[256]{0:T(512)(128)(4,1)S(1)} %compare_and_fusion, pred[512]{0:T(512)(128)(4,1)S(1)} %get-tuple-element.51, ...), kind=kLoop, calls=%fused_computation.32 | loop fusion | flops 3538944 | bytes 532224 | tf_op jit(solution)/shard_map/jit(_where)/select_n | solution.py:37
  18.4 6.1 %collective-permute-start.6 = (bf16[1280,128]{1,0:T(8,128)(2,1)S(1)}, bf16[1280,128]{1,0:T(8,128)(2,1)}, u32[]{:S(2)}, u32[]{:S(2)}) collective-permute-start(bf16[1280,128]{1,0:T(8,128)(2,1)S(1)} %get-tuple-element.16), channel_id=1, source_target_pairs={{0,224},{32,0},{64,32},{96,64},{128,96},{160,128},{192,160},{224,1... | collective-permute-start | bytes 983048 | tf_op jit(solution)/shard_map/ppermute | solution.py:115
  27.7 2.7 %collective-permute-start = (bf16[1280,128]{1,0:T(8,128)(2,1)S(1)}, bf16[1280,128]{1,0:T(8,128)(2,1)}, u32[]{:S(2)}, u32[]{:S(2)}) collective-permute-start(bf16[1280,128]{1,0:T(8,128)(2,1)S(1)} %get-tuple-element.16), channel_id=1, source_target_pairs={{0,32},{32,64},{64,96},{96,128},{128,160},{160,192},{192,224},{224... | collective-permute-start | bytes 983048 | tf_op jit(solution)/shard_map/ppermute | solution.py:115
  34.2 11.8 %collective-permute-done = bf16[1280,128]{1,0:T(8,128)(2,1)} collective-permute-done((bf16[1280,128]{1,0:T(8,128)(2,1)S(1)}, bf16[1280,128]{1,0:T(8,128)(2,1)}, u32[]{:S(2)}, u32[]{:S(2)}) %collective-permute-start) | collective-permute-done | bytes 327712 | tf_op jit(solution)/shard_map/ppermute | solution.py:115
  47.1 7.9 %collective-permute-done.1 = bf16[1280,128]{1,0:T(8,128)(2,1)S(1)} collective-permute-done((bf16[1280,128]{1,0:T(8,128)(2,1)S(1)}, bf16[1280,128]{1,0:T(8,128)(2,1)S(1)}, u32[]{:S(2)}, u32[]{:S(2)}) %collective-permute-start.1) | collective-permute-done | bytes 327712 | tf_op jit(solution)/shard_map/ppermute | solution.py:115
  56.7 9.0 %collective-permute-done.2 = bf16[1280,128]{1,0:T(8,128)(2,1)S(1)} collective-permute-done((bf16[1280,128]{1,0:T(8,128)(2,1)S(1)}, bf16[1280,128]{1,0:T(8,128)(2,1)S(1)}, u32[]{:S(2)}, u32[]{:S(2)}) %collective-permute-start.2) | collective-permute-done | bytes 327712 | tf_op jit(solution)/shard_map/ppermute | solution.py:115
  70.8 3.0 %collective-permute-start.11 = (bf16[1280,128]{1,0:T(8,128)(2,1)S(1)}, bf16[1280,128]{1,0:T(8,128)(2,1)}, u32[]{:S(2)}, u32[]{:S(2)}) collective-permute-start(bf16[1280,128]{1,0:T(8,128)(2,1)S(1)} %get-tuple-element.22), channel_id=1, source_target_pairs={{0,160},{32,192},{64,224},{96,0},{128,32},{160,64},{192,96},{224,1... | collective-permute-start | bytes 983048 | tf_op jit(solution)/shard_map/ppermute | solution.py:115
  75.7 2.7 %collective-permute-start.7 = (bf16[1280,128]{1,0:T(8,128)(2,1)S(1)}, bf16[1280,128]{1,0:T(8,128)(2,1)}, u32[]{:S(2)}, u32[]{:S(2)}) collective-permute-start(bf16[1280,128]{1,0:T(8,128)(2,1)S(1)} %get-tuple-element.22), channel_id=1, source_target_pairs={{0,32},{32,64},{64,96},{96,128},{128,160},{160,192},{192,224},{224... | collective-permute-start | bytes 983048 | tf_op jit(solution)/shard_map/ppermute | solution.py:115
  87.4 3.2 %copy.10 = bf16[512,8,3,128]{0,3,2,1:T(8,128)(2,1)S(1)} copy(bf16[512,8,3,128]{3,0,2,1:T(8,128)(2,1)} %pad_maximum_fusion) | data formatting | bytes 6291456 | tf_op jit(solution)/shard_map/concatenate | solution.py:131
  90.6 5.7 %fusion.56.seg_re.seg_im = f32[512,3072]{1,0:T(8,128)} fusion(bf16[512,512]{1,0:T(8,128)(2,1)} %select_convert_fusion, bf16[512,3072]{0,1:T(8,128)(2,1)S(1)} %bitcast.78), kind=kOutput, calls=%fused_computation.127 | convolution fusion | flops 1610612736 | bytes 9961472 | tf_op jit(solution)/shard_map/dot_general | solution.py:139
  96.3 2.8 %fusion.26.sp_re.sp_im = f32[512,2048]{1,0:T(8,128)} fusion(bf16[256,2048]{0,1:T(8,128)(2,1)S(1)} %bitcast.84, bf16[512,512]{1,0:T(8,128)(2,1)S(1)} %copy-done.3), kind=kOutput, calls=%fused_computation.69 | convolution fusion | flops 536870912 | bytes 5505024 | tf_op jit(solution)/shard_map/dot_general | solution.py:141
  99.1 9.5 %shard_map.95 = (f32[256,384]{1,0:T(8,128)}, f32[256,384]{1,0:T(8,128)}) custom-call(s32[48]{0:T(128)} %fusion.43.lag_ref, s32[48]{0:T(128)} %reshape.241.ok_ref, f32[512,3072]{1,0:T(8,128)} %fusion.56.seg_re.seg_im, f32[512,3072]{1,0:T(8,128)} %fusion.56.seg_re.seg_im, f32[512,2048]{1,0:T(8,128)} %fusion.26.sp_re.sp_im, f32[512,2048]{1,0:T(8,128)} %fusion.26.sp_re.sp_im), custom_call_target="tpu_custom_call" | custom-call | tf_op jit(solution)/shard_map/pallas_call | solution.py:87
  113.8 5.3 %collective-permute-done.8 = bf16[1280,128]{1,0:T(8,128)(2,1)S(1)} collective-permute-done((bf16[1280,128]{1,0:T(8,128)(2,1)S(1)}, bf16[1280,128]{1,0:T(8,128)(2,1)S(1)}, u32[]{:S(2)}, u32[]{:S(2)}) %collective-permute-start.8) | collective-permute-done | bytes 327712 | tf_op jit(solution)/shard_map/ppermute | solution.py:115
  119.1 9.8 %collective-permute-done.9 = bf16[1280,128]{1,0:T(8,128)(2,1)S(1)} collective-permute-done((bf16[1280,128]{1,0:T(8,128)(2,1)S(1)}, bf16[1280,128]{1,0:T(8,128)(2,1)S(1)}, u32[]{:S(2)}, u32[]{:S(2)}) %collective-permute-start.9) | collective-permute-done | bytes 327712 | tf_op jit(solution)/shard_map/ppermute | solution.py:115
  139.9 3.2 %copy.12 = bf16[512,8,3,128]{0,3,2,1:T(8,128)(2,1)S(1)} copy(bf16[512,8,3,128]{3,0,2,1:T(8,128)(2,1)} %pad_maximum_fusion.1) | data formatting | bytes 6291456 | tf_op jit(solution)/shard_map/concatenate | solution.py:131
  143.1 5.7 %fusion.57.seg_re.seg_im = f32[512,3072]{1,0:T(8,128)} fusion(bf16[512,512]{1,0:T(8,128)(2,1)} %select_convert_fusion, bf16[512,3072]{0,1:T(8,128)(2,1)S(1)} %bitcast.79), kind=kOutput, calls=%fused_computation.128 | convolution fusion | flops 1610612736 | bytes 9961472 | tf_op jit(solution)/shard_map/dot_general | solution.py:139
  148.8 2.8 %fusion.24.sp_re.sp_im = f32[512,2048]{1,0:T(8,128)} fusion(bf16[256,2048]{0,1:T(8,128)(2,1)S(1)} %bitcast.83, bf16[512,512]{1,0:T(8,128)(2,1)S(1)} %copy-done.4), kind=kOutput, calls=%fused_computation.66 | convolution fusion | flops 536870912 | bytes 5505024 | tf_op jit(solution)/shard_map/dot_general | solution.py:141
  151.6 9.5 %shard_map.96 = (f32[256,384]{1,0:T(8,128)}, f32[256,384]{1,0:T(8,128)}) custom-call(s32[48]{0:T(128)} %fusion.43.lag_ref, s32[48]{0:T(128)} %reshape.241.ok_ref, f32[512,3072]{1,0:T(8,128)} %fusion.57.seg_re.seg_im, f32[512,3072]{1,0:T(8,128)} %fusion.57.seg_re.seg_im, f32[512,2048]{1,0:T(8,128)} %fusion.24.sp_re.sp_im, f32[512,2048]{1,0:T(8,128)} %fusion.24.sp_re.sp_im), custom_call_target="tpu_custom_call" | custom-call | tf_op jit(solution)/shard_map/pallas_call | solution.py:87
  163.2 5.2 %collective-permute-done.14 = bf16[512,256]{1,0:T(8,128)(2,1)S(1)} collective-permute-done((bf16[512,256]{1,0:T(8,128)(2,1)S(1)}, bf16[512,256]{1,0:T(8,128)(2,1)S(1)}, u32[]{:S(2)}, u32[]{:S(2)}) %collective-permute-start.14) | collective-permute-done | bytes 262176 | tf_op jit(solution)/shard_map/ppermute | solution.py:94
  169.4 61.6 %all-gather.2.cloned.1.call-done = bf16[512,4096]{1,0:T(8,128)(2,1)} async-done(((bf16[512,512]{1,0:T(8,128)(2,1)}), bf16[512,4096]{1,0:T(8,128)(2,1)}) %all-gather.2.cloned.1.call-update) | async-done | bytes 4194320 | tf_op jit(solution)/shard_map/all_gather | solution.py:211
  231.8 2.7 %constant_dynamic-slice_fusion.1 = (bf16[8,2,1,256,256]{4,3,2,1,0:T(8,128)(2,1)S(1)}, bf16[8,2,1,256,256]{4,3,2,1,0:T(8,128)(2,1)S(1)}) fusion(bf16[8,2,2,256,256]{4,3,2,1,0:T(8,128)(2,1)} %bitcast.80, s32[]{:T(128)S(6)} %select_n.232, s32[]{:T(128)S(6)} %select_n.233), kind=kLoop, calls=%fused_computation.120 | loop fusion | bytes 8388616 | tf_op jit(solution)/shard_map/jit(dynamic_index_in_dim)/dynamic_slice | solution.py:180
  235.2 3.7 %collective-permute-done.15 = bf16[512,4096]{1,0:T(8,128)(2,1)} collective-permute-done((bf16[512,4096]{1,0:T(8,128)(2,1)}, bf16[512,4096]{1,0:T(8,128)(2,1)}, u32[]{:S(2)}, u32[]{:S(2)}) %collective-permute-start.15) | collective-permute-done | bytes 4194336 | tf_op jit(solution)/shard_map/ppermute | solution.py:94
  238.9 3.6 %fusion.58 = f32[512,256]{1,0:T(8,128)S(1)} fusion(bf16[512,4096]{1,0:T(8,128)(2,1)} %collective-permute-done.15, bf16[4096,256]{1,0:T(8,128)(2,1)S(1)} %bitcast.86), kind=kOutput, calls=%fused_computation.129 | convolution fusion | flops 1073741824 | bytes 6815744 | tf_op jit(solution)/shard_map/dot_general | solution.py:212
  (133 shorter events, 50.1 us)
Async XLA Ops:
  7.2 223.8 %all-gather.2.cloned.1.call-start = ((), (), s32[]{:S(2)}) async-start(), calls=%async_computation | async-start | bytes 4718592 | tf_op jit(solution)/shard_map/all_gather | solution.py:211
  7.3 23.2 %copy-start = (s32[16]{0:T(128)S(1)}, s32[16]{0:T(128)}, u32[]{:S(2)}) copy-start(s32[16]{0:T(128)} %param.14) | copy-start | bytes 196
  8.5 22.8 %copy-start.19 = (s32[8]{0:T(128)S(1)}, s32[8]{0:T(128)}, u32[]{:S(2)}) copy-start(s32[8]{0:T(128)} %param.15) | copy-start | bytes 100
  8.5 24.2 %copy-start.17 = (f32[256]{0:T(256)S(1)}, f32[256]{0:T(256)}, u32[]{:S(2)}) copy-start(f32[256]{0:T(256)} %param.12) | copy-start | bytes 3076
  9.7 22.9 %copy-start.11 = (bf16[512,128]{1,0:T(8,128)(2,1)}, bf16[512,128]{1,0:T(8,128)(2,1)S(1)}, u32[]{:S(2)}) copy-start(bf16[512,128]{1,0:T(8,128)(2,1)S(1)} %get-tuple-element.28) | copy-start | bytes 393220
  9.7 46.9 %copy-start.9 = (bf16[512,128]{1,0:T(8,128)(2,1)}, bf16[512,128]{1,0:T(8,128)(2,1)S(1)}, u32[]{:S(2)}) copy-start(bf16[512,128]{1,0:T(8,128)(2,1)S(1)} %get-tuple-element.29) | copy-start | bytes 393220
  18.4 50.4 %collective-permute-start.6 = (bf16[1280,128]{1,0:T(8,128)(2,1)S(1)}, bf16[1280,128]{1,0:T(8,128)(2,1)}, u32[]{:S(2)}, u32[]{:S(2)}) collective-permute-start(bf16[1280,128]{1,0:T(8,128)(2,1)S(1)} %get-tuple-element.16), channel_id=1, source_target_pairs={{0,224},{32,0},{64,32},{96,64},{128,96},{160,128},{192,160},{224,1... | collective-permute-start | bytes 983048 | tf_op jit(solution)/shard_map/ppermute | solution.py:115
  24.5 43.3 %collective-permute-start.5 = (bf16[1280,128]{1,0:T(8,128)(2,1)S(1)}, bf16[1280,128]{1,0:T(8,128)(2,1)}, u32[]{:S(2)}, u32[]{:S(2)}) collective-permute-start(bf16[1280,128]{1,0:T(8,128)(2,1)S(1)} %get-tuple-element.16), channel_id=1, source_target_pairs={{0,192},{32,224},{64,0},{96,32},{128,64},{160,96},{192,128},{224,1... | collective-permute-start | bytes 983048 | tf_op jit(solution)/shard_map/ppermute | solution.py:115
  25.0 41.8 %collective-permute-start.4 = (bf16[1280,128]{1,0:T(8,128)(2,1)S(1)}, bf16[1280,128]{1,0:T(8,128)(2,1)}, u32[]{:S(2)}, u32[]{:S(2)}) collective-permute-start(bf16[1280,128]{1,0:T(8,128)(2,1)S(1)} %get-tuple-element.16), channel_id=1, source_target_pairs={{0,160},{32,192},{64,224},{96,0},{128,32},{160,64},{192,96},{224,1... | collective-permute-start | bytes 983048 | tf_op jit(solution)/shard_map/ppermute | solution.py:115
  25.1 40.6 %collective-permute-start.3 = (bf16[1280,128]{1,0:T(8,128)(2,1)S(1)}, bf16[1280,128]{1,0:T(8,128)(2,1)}, u32[]{:S(2)}, u32[]{:S(2)}) collective-permute-start(bf16[1280,128]{1,0:T(8,128)(2,1)S(1)} %get-tuple-element.16), channel_id=1, source_target_pairs={{0,128},{32,160},{64,192},{96,224},{128,0},{160,32},{192,64},{224,... | collective-permute-start | bytes 983048 | tf_op jit(solution)/shard_map/ppermute | solution.py:115
  27.7 18.3 %collective-permute-start = (bf16[1280,128]{1,0:T(8,128)(2,1)S(1)}, bf16[1280,128]{1,0:T(8,128)(2,1)}, u32[]{:S(2)}, u32[]{:S(2)}) collective-permute-start(bf16[1280,128]{1,0:T(8,128)(2,1)S(1)} %get-tuple-element.16), channel_id=1, source_target_pairs={{0,32},{32,64},{64,96},{96,128},{128,160},{160,192},{192,224},{224... | collective-permute-start | bytes 983048 | tf_op jit(solution)/shard_map/ppermute | solution.py:115
  46.0 8.9 %collective-permute-start.1 = (bf16[1280,128]{1,0:T(8,128)(2,1)S(1)}, bf16[1280,128]{1,0:T(8,128)(2,1)S(1)}, u32[]{:S(2)}, u32[]{:S(2)}) collective-permute-start(bf16[1280,128]{1,0:T(8,128)(2,1)S(1)} %get-tuple-element.16), channel_id=1, source_target_pairs={{0,64},{32,96},{64,128},{96,160},{128,192},{160,224},{192,0},{224,... | collective-permute-start | bytes 983048 | tf_op jit(solution)/shard_map/ppermute | solution.py:115
  54.9 10.7 %collective-permute-start.2 = (bf16[1280,128]{1,0:T(8,128)(2,1)S(1)}, bf16[1280,128]{1,0:T(8,128)(2,1)S(1)}, u32[]{:S(2)}, u32[]{:S(2)}) collective-permute-start(bf16[1280,128]{1,0:T(8,128)(2,1)S(1)} %get-tuple-element.16), channel_id=1, source_target_pairs={{0,96},{32,128},{64,160},{96,192},{128,224},{160,0},{192,32},{224,... | collective-permute-start | bytes 983048 | tf_op jit(solution)/shard_map/ppermute | solution.py:115
  69.9 62.2 %collective-permute-start.13 = (bf16[1280,128]{1,0:T(8,128)(2,1)S(1)}, bf16[1280,128]{1,0:T(8,128)(2,1)}, u32[]{:S(2)}, u32[]{:S(2)}) collective-permute-start(bf16[1280,128]{1,0:T(8,128)(2,1)S(1)} %get-tuple-element.22), channel_id=1, source_target_pairs={{0,224},{32,0},{64,32},{96,64},{128,96},{160,128},{192,160},{224,1... | collective-permute-start | bytes 983048 | tf_op jit(solution)/shard_map/ppermute | solution.py:115
  70.4 60.5 %collective-permute-start.12 = (bf16[1280,128]{1,0:T(8,128)(2,1)S(1)}, bf16[1280,128]{1,0:T(8,128)(2,1)}, u32[]{:S(2)}, u32[]{:S(2)}) collective-permute-start(bf16[1280,128]{1,0:T(8,128)(2,1)S(1)} %get-tuple-element.22), channel_id=1, source_target_pairs={{0,192},{32,224},{64,0},{96,32},{128,64},{160,96},{192,128},{224,1... | collective-permute-start | bytes 983048 | tf_op jit(solution)/shard_map/ppermute | solution.py:115
  70.8 59.2 %collective-permute-start.11 = (bf16[1280,128]{1,0:T(8,128)(2,1)S(1)}, bf16[1280,128]{1,0:T(8,128)(2,1)}, u32[]{:S(2)}, u32[]{:S(2)}) collective-permute-start(bf16[1280,128]{1,0:T(8,128)(2,1)S(1)} %get-tuple-element.22), channel_id=1, source_target_pairs={{0,160},{32,192},{64,224},{96,0},{128,32},{160,64},{192,96},{224,1... | collective-permute-start | bytes 983048 | tf_op jit(solution)/shard_map/ppermute | solution.py:115
  73.8 55.2 %collective-permute-start.10 = (bf16[1280,128]{1,0:T(8,128)(2,1)S(1)}, bf16[1280,128]{1,0:T(8,128)(2,1)}, u32[]{:S(2)}, u32[]{:S(2)}) collective-permute-start(bf16[1280,128]{1,0:T(8,128)(2,1)S(1)} %get-tuple-element.22), channel_id=1, source_target_pairs={{0,128},{32,160},{64,192},{96,224},{128,0},{160,32},{192,64},{224,... | collective-permute-start | bytes 983048 | tf_op jit(solution)/shard_map/ppermute | solution.py:115
  75.7 36.3 %collective-permute-start.7 = (bf16[1280,128]{1,0:T(8,128)(2,1)S(1)}, bf16[1280,128]{1,0:T(8,128)(2,1)}, u32[]{:S(2)}, u32[]{:S(2)}) collective-permute-start(bf16[1280,128]{1,0:T(8,128)(2,1)S(1)} %get-tuple-element.22), channel_id=1, source_target_pairs={{0,32},{32,64},{64,96},{96,128},{128,160},{160,192},{192,224},{224... | collective-permute-start | bytes 983048 | tf_op jit(solution)/shard_map/ppermute | solution.py:115
  99.1 12.1 %copy-start.12 = (bf16[512,128]{1,0:T(8,128)(2,1)S(1)}, bf16[512,128]{1,0:T(8,128)(2,1)}, u32[]{:S(2)}) copy-start(bf16[512,128]{1,0:T(8,128)(2,1)} %copy-done.11) | copy-start | bytes 393220
  99.1 12.1 %copy-start.15 = (bf16[512,256]{1,0:T(8,128)(2,1)S(1)}, bf16[512,256]{1,0:T(8,128)(2,1)}, u32[]{:S(2)}) copy-start(bf16[512,256]{1,0:T(8,128)(2,1)} %param.8) | copy-start | bytes 786436
  111.9 7.1 %collective-permute-start.8 = (bf16[1280,128]{1,0:T(8,128)(2,1)S(1)}, bf16[1280,128]{1,0:T(8,128)(2,1)S(1)}, u32[]{:S(2)}, u32[]{:S(2)}) collective-permute-start(bf16[1280,128]{1,0:T(8,128)(2,1)S(1)} %get-tuple-element.22), channel_id=1, source_target_pairs={{0,64},{32,96},{64,128},{96,160},{128,192},{160,224},{192,0},{224,... | collective-permute-start | bytes 983048 | tf_op jit(solution)/shard_map/ppermute | solution.py:115
  119.0 9.8 %collective-permute-start.9 = (bf16[1280,128]{1,0:T(8,128)(2,1)S(1)}, bf16[1280,128]{1,0:T(8,128)(2,1)S(1)}, u32[]{:S(2)}, u32[]{:S(2)}) collective-permute-start(bf16[1280,128]{1,0:T(8,128)(2,1)S(1)} %get-tuple-element.22), channel_id=1, source_target_pairs={{0,96},{32,128},{64,160},{96,192},{128,224},{160,0},{192,32},{224,... | collective-permute-start | bytes 983048 | tf_op jit(solution)/shard_map/ppermute | solution.py:115
  163.1 5.3 %collective-permute-start.14 = (bf16[512,256]{1,0:T(8,128)(2,1)S(1)}, bf16[512,256]{1,0:T(8,128)(2,1)S(1)}, u32[]{:S(2)}, u32[]{:S(2)}) collective-permute-start(bf16[512,256]{1,0:T(8,128)(2,1)S(1)} %pad_maximum_fusion.6), channel_id=1, source_target_pairs={{0,2},{2,0},{1,3},{3,1},{4,6},{6,4},{5,7},{7,5},{8,10},{10,8},{9,1... | collective-permute-start | bytes 786440 | tf_op jit(solution)/shard_map/ppermute | solution.py:94
  231.0 8.0 %collective-permute-start.15 = (bf16[512,4096]{1,0:T(8,128)(2,1)}, bf16[512,4096]{1,0:T(8,128)(2,1)}, u32[]{:S(2)}, u32[]{:S(2)}) collective-permute-start(bf16[512,4096]{1,0:T(8,128)(2,1)} %all-gather.2.cloned.1.call-done), channel_id=1, source_target_pairs={{0,1},{1,0},{2,3},{3,2},{4,5},{5,4},{6,7},{7,6},{8,9},{9,8},{10,11... | collective-permute-start | bytes 12582920 | tf_op jit(solution)/shard_map/ppermute | solution.py:94
  (13 other events, 85.4 us)
Sparse Core Ops, SparseCore 0:
  169.5 61.3 all-gather.1
